TPU v7x, 256 devices: a whole 4x4x8 slice. The times are simulated.
256 devices in a mesh: tm: 64 (over z, x_hi, y), chan: 4 (over x_lo, core).
Axes of the slice: x: 4 (x_hi: 2, x_lo: 2; x = x_hi * 2 + x_lo), y: 4, z: 8, core: 2. Of those that a mesh axis runs over, the one named last changes fastest.
Arguments:
- signal: float32 [256, 8192], P('chan', 'tm'), may hold values from -256 to 256
- support: int32 [32], replicated, may hold values from 1 to 4, as said below
- pair_first: int32 [4, 512], replicated, may hold values from 0 to 255
- pair_second: int32 [4, 512], replicated, may hold values from 0 to 255
- pair_count: int32 [4], replicated, may hold values from 128 to 512, as said below
Outputs:
- cross: float32 [4, 512, 2, 32], P('chan', 'tm')
- coherence: float32 [4, 512, 32], P('chan', 'tm')
Inputs may be any that keep to these rules, and one draw needn't show every extreme that they name: With b = q // 8 the band of scale q, support[q] is at most (4 * 128 / 4^(3 - b) + 127) // 128, and equals it for the last scale of every band. The live slots of an owner are its first pair_count slots; some owner has all 512 slots live.
All inputs are finite; a program needn't handle non-finite values.
Results may differ from a plain program's by a relative error of at most 0.0027.
Values may be sent and summed in bfloat16 or wider, within the bound.
No kernel may reach another device: no remote copies, remote signals or barrier semaphores. Data moves between devices by JAX's collectives and lax.ppermute only.
A program may use at most 192 MiB of HBM per device.

v0:
```python
import math
import jax
import jax.numpy as jnp
import numpy as np
from jax import lax
from jax.sharding import PartitionSpec as P

NS = 32
BLK = 128
TD = 128
power_floor = 1e-06


def from_behind(array, axis, by):
    peers = lax.axis_size(axis)
    return lax.ppermute(array, axis, [(i, (i + by) % peers) for i in range(peers)])


def kernel_table(scale_ids, reaches, offsets):
    taps = (2 * offsets + 1) * BLK
    lag = jnp.arange(taps, dtype=jnp.int32) - offsets * BLK
    within = jnp.arange(BLK, dtype=jnp.int32)
    scale_width = 2.0 * TD * jnp.exp2((scale_ids - (NS - 1)).astype(jnp.float32) / 4.0)
    width = scale_width[:, None, None]
    offset = lag[None, :, None] - within[None, None, :]
    scaled_offset = offset.astype(jnp.float32) / width
    amplitude = (
        math.pi ** (-0.25) * lax.rsqrt(width) * jnp.exp(-0.5 * scaled_offset * scaled_offset)
    )
    inside = jnp.abs(offset) < (reaches * BLK)[:, None, None]
    lag_phase = 6.0 * (lag.astype(jnp.float32)[None, :] / scale_width[:, None])
    time_phase = 6.0 * (within.astype(jnp.float32)[None, :] / scale_width[:, None])
    lag_cos = jnp.cos(lag_phase)[:, :, None]
    lag_sin = jnp.sin(lag_phase)[:, :, None]
    time_cos = jnp.cos(time_phase)[:, None, :]
    time_sin = jnp.sin(time_phase)[:, None, :]
    cos_part = lag_cos * time_cos + lag_sin * time_sin
    sin_part = lag_sin * time_cos - lag_cos * time_sin
    real_part = jnp.where(inside, amplitude * cos_part, 0.0).astype(jnp.bfloat16)
    imag_part = jnp.where(inside, amplitude * sin_part, 0.0).astype(jnp.bfloat16)
    return jnp.stack([real_part, imag_part], axis=1)


def band_coefficients(extended, scale_ids, reaches, offsets):
    channels = extended.shape[0]
    table = kernel_table(scale_ids, reaches, offsets)
    coefficients = jnp.einsum("cm,qrmt->qrct", extended, table, preferred_element_type=jnp.float32)
    scale_count = scale_ids.shape[0]
    return coefficients.astype(jnp.bfloat16).reshape(scale_count, 2 * channels, BLK)


def pair_sums(coefficients, first_flat, second_flat):
    scale_count = coefficients.shape[0]
    channels = coefficients.shape[1] // 2
    time_span = coefficients.shape[2]
    chan_iota = jnp.arange(channels, dtype=jnp.int32)
    both = jnp.concatenate([first_flat, second_flat])
    pick = (both[:, None] == chan_iota[None, :]).astype(jnp.bfloat16)
    parts = coefficients.reshape(scale_count, 2, channels, time_span)
    picked = jnp.einsum("pc,qrct->qrpt", pick, parts, preferred_element_type=jnp.bfloat16)
    pairs = first_flat.shape[0]
    first_real = picked[:, 0, :pairs]
    first_imag = picked[:, 1, :pairs]
    second_real = picked[:, 0, pairs:]
    second_imag = picked[:, 1, pairs:]

    def time_sum(left, right):
        return jnp.einsum("qpt,qpt->qp", left, right, preferred_element_type=jnp.float32)

    cross_real = time_sum(first_real, second_real) + time_sum(first_imag, second_imag)
    cross_imag = time_sum(first_imag, second_real) - time_sum(first_real, second_imag)
    power = jnp.einsum("qrct,qrct->qc", parts, parts, preferred_element_type=jnp.float32)
    high = lax.reduce_precision(power, exponent_bits=8, mantissa_bits=7)
    rest = power - high
    middle = lax.reduce_precision(rest, exponent_bits=8, mantissa_bits=7)
    low = rest - middle
    pieces = jnp.stack([high, middle, low]).astype(jnp.bfloat16)
    picked_power = jnp.einsum("pc,kqc->kqp", pick, pieces, preferred_element_type=jnp.float32)
    owner_power = picked_power[0] + picked_power[1] + picked_power[2]
    power_first = owner_power[:, :pairs]
    power_second = owner_power[:, pairs:]
    return jnp.stack([cross_real, cross_imag, power_first, power_second], axis=1)


def shards(signal, support, pair_first, pair_second, pair_count):
    groups = lax.axis_size("chan")
    cluster_number = lax.axis_index("chan")
    time_index = lax.axis_index("tm")
    time_devices = lax.axis_size("tm")
    time_span = signal.shape[1]
    ntime = time_span * time_devices
    rounded = signal.astype(jnp.bfloat16)
    gathered = lax.all_gather(rounded, "chan", axis=0, tiled=True)
    near = jnp.concatenate(
        [from_behind(gathered, "tm", 1), gathered, from_behind(gathered, "tm", -1)], axis=1
    )
    wide = jnp.concatenate([from_behind(near, "tm", 3), near, from_behind(near, "tm", -3)], axis=1)
    per_group = NS // groups
    band = NS // 4
    narrow_count = (NS - band) // groups
    wide_count = band // groups
    narrow_ids = cluster_number * narrow_count + jnp.arange(narrow_count, dtype=jnp.int32)
    wide_ids = NS - band + cluster_number * wide_count + jnp.arange(wide_count, dtype=jnp.int32)
    narrow_coefficients = band_coefficients(near, narrow_ids, support[narrow_ids], 1)
    wide_coefficients = band_coefficients(wide, wide_ids, support[wide_ids], 4)
    owner_devices, slots_total = pair_first.shape
    slots_local = slots_total // time_devices

    def by_block(pairs):
        return (
            pairs.reshape(owner_devices, time_devices, slots_local).transpose(2, 1, 0).reshape(-1)
        )

    first_flat = by_block(pair_first)
    second_flat = by_block(pair_second)
    sums = jnp.concatenate(
        [
            pair_sums(narrow_coefficients, first_flat, second_flat),
            pair_sums(wide_coefficients, first_flat, second_flat),
        ],
        axis=0,
    )
    values = sums.shape[1]
    destinations = time_devices * groups
    partial_value = sums.reshape(per_group * values * slots_local, destinations).T
    partial_value = partial_value.reshape(destinations, 2, -1)
    exchanged = lax.all_to_all(partial_value, ("tm", "chan"), 0, 0, tiled=True)
    summed = jnp.sum(exchanged.reshape(time_devices, groups, -1), axis=0)
    owned = summed.reshape(groups, per_group, values, slots_local) / ntime
    owned = owned.reshape(groups, per_group, values, slots_local)
    owned = jnp.concatenate(
        [
            owned[:, :narrow_count].reshape(groups * narrow_count, values, slots_local),
            owned[:, narrow_count:].reshape(groups * wide_count, values, slots_local),
        ],
        axis=0,
    )
    slot_index = time_index * slots_local + jnp.arange(slots_local, dtype=jnp.int32)
    alive_mask = slot_index < pair_count[cluster_number]
    cross_real = owned[:, 0, :].T
    cross_imag = owned[:, 1, :].T
    first_power = owned[:, 2, :].T
    second_power = owned[:, 3, :].T
    coherence = (cross_real * cross_real + cross_imag * cross_imag) / (
        (first_power + power_floor) * (second_power + power_floor)
    )
    coherence = jnp.where(alive_mask[:, None], coherence, 0.0)[None]
    cross = jnp.stack([cross_real, cross_imag], axis=1)
    cross = jnp.where(alive_mask[:, None, None], cross, 0.0)[None]
    return (cross, coherence.astype(jnp.float32))


def solution(mesh):
    in_specs = (P("chan", "tm"), P(), P(), P(), P())
    out_specs = (P("chan", "tm", None, None), P("chan", "tm", None))
    return jax.shard_map(shards, mesh=mesh, in_specs=in_specs, out_specs=out_specs, check_vma=False)
```

profile of v0, /device:TPU:1, one launch (start us, length us, event | category | flops | bytes accessed | tf_op | source)
XLA Modules:
  0.0 72.6 jit_solution(3698254476402934474)
XLA Ops:
  0.7 0.8 %convert_element_type.133 = bf16[64,128]{1,0:T(8,128)(2,1)S(1)} convert(f32[64,128]{1,0:T(8,128)} %param.5) | non-fusion elementwise | flops 8192 | bytes 49152 | tf_op jit(solution)/shard_map/convert_element_type | solution.py:92
  1.4 8.3 %all_gather.3 = bf16[256,128]{1,0:T(8,128)(2,1)S(1)} all-gather(bf16[64,128]{1,0:T(8,128)(2,1)S(1)} %convert_element_type.133), channel_id=1, replica_groups=mesh['tm'=64,'chan'=4] {'chan'}, dimensions={0}, use_global_device_ids=true | all-gather | bytes 81920 | tf_op jit(solution)/shard_map/all_gather | solution.py:93
  9.7 8.8 %collective-permute-start.1 = (bf16[256,128]{1,0:T(8,128)(2,1)S(1)}, bf16[256,128]{1,0:T(8,128)(2,1)S(1)}, u32[]{:S(2)}, u32[]{:S(2)}) collective-permute-start(bf16[256,128]{1,0:T(8,128)(2,1)S(1)} %all_gather.3), channel_id=1, source_target_pairs={{0,252},{4,0},{8,4},{12,8},{16,12},{20,16},{24,20},{28,24},{32,28}... | collective-permute-start | bytes 196616 | tf_op jit(solution)/shard_map/ppermute | solution.py:16
  18.6 0.6 gather_fusion.1
  19.3 0.6 gather_fusion
  22.3 0.8 %fusion.25 = (bf16[6,1,384,128]{2,3,1,0:T(8,128)(2,1)S(1)}, bf16[6,1,384,128]{2,3,1,0:T(8,128)(2,1)S(1)}) fusion(f32[6,128]{1,0:T(8,128)S(1)} %get-tuple-element.43, f32[6,384]{1,0:T(8,128)S(1)} %get-tuple-element.36, f32[6,128]{1,0:T(8,128)S(1)} %get-tuple-element.42, f32[6,384]{1,0:T(8,128)S(1)} %get-tuple-element.35, f32[6]{0:T(128)S(1)} %get-tuple-element.55, ...), kind=kLoop, calls=%fused_computation.47 | loop fusion | flops 5013504 | bytes 1597512 | tf_op jit(solution)/shard_map/convert_element_type | solution.py:39
  23.1 1.0 %fusion.27 = (bf16[2,1,1152,128]{2,3,1,0:T(8,128)(2,1)S(1)}, bf16[2,1,1152,128]{2,3,1,0:T(8,128)(2,1)S(1)}) fusion(f32[2,128]{1,0:T(2,128)S(1)} %get-tuple-element.45, f32[2,1152]{1,0:T(2,128)S(1)} %get-tuple-element.29, f32[2,128]{1,0:T(2,128)S(1)} %get-tuple-element.44, f32[2,1152]{1,0:T(2,128)S(1)} %get-tuple-element.28, f32[2]{0:T(128)S(1)} %get-tuple-element.51, ...), kind=kLoop, calls=%fused_computation.49 | loop fusion | flops 5013504 | bytes 2379800 | tf_op jit(solution)/shard_map/convert_element_type | solution.py:39
  24.0 3.3 %collective-permute-done = bf16[256,128]{1,0:T(8,128)(2,1)S(1)} collective-permute-done((bf16[256,128]{1,0:T(8,128)(2,1)S(1)}, bf16[256,128]{1,0:T(8,128)(2,1)S(1)}, u32[]{:S(2)}, u32[]{:S(2)}) %collective-permute-start) | collective-permute-done | bytes 65568 | tf_op jit(solution)/shard_map/ppermute | solution.py:16
  27.5 2.7 %collective-permute-start.2 = (bf16[256,384]{1,0:T(8,128)(2,1)S(1)}, bf16[256,384]{1,0:T(8,128)(2,1)S(1)}, u32[]{:S(2)}, u32[]{:S(2)}) collective-permute-start(bf16[256,384]{1,0:T(8,128)(2,1)S(1)} %constant_dynamic-update-slice_fusion), channel_id=1, source_target_pairs={{0,12},{4,16},{8,20},{12,24},{16,28},{20,32},{24,36},{28,40},{32,4... | collective-permute-start | bytes 589832 | tf_op jit(solution)/shard_map/ppermute | solution.py:16
  30.2 0.6 fusion.20
  30.8 0.8 %fusion.10 = f32[3,6,4096]{2,1,0:T(8,128)S(1)} fusion(s32[4096]{0:T(1024)S(1)} %pad_add_fusion, bf16[1,6,256]{2,1,0:T(8,128)(2,1)S(1)} %get-tuple-element.31, bf16[1,6,256]{2,1,0:T(8,128)(2,1)S(1)} %get-tuple-element.32, bf16[1,6,256]{2,1,0:T(8,128)(2,1)S(1)} %get-tuple-element.30), kind=kOutput, calls=%fused_computation.16 | convolution fusion | flops 38806528 | bytes 320512 | tf_op jit(solution)/shard_map/pc,kqc->kqp/dot_general | solution.py:78
  31.7 3.9 %convolution_bitcast_fusion = bf16[6,2,4096,128]{2,3,1,0:T(8,128)(2,1)S(1)} fusion(s32[4096]{0:T(1024)S(1)} %pad_add_fusion, bf16[6,2,128,256]{3,2,1,0:T(8,128)(2,1)S(1)} %get-tuple-element.49), kind=kOutput, calls=%fused_computation.6 | convolution fusion | flops 3222274048 | bytes 13385728 | tf_op jit(solution)/shard_map/pc,qrct->qrpt/dot_general | solution.py:60
  35.6 3.1 %fusion.2 = (f32[6,2048]{1,0:T(8,128)S(1)}, f32[6,2048]{1,0:T(8,128)S(1)}, f32[6,2048]{1,0:T(8,128)S(1)}, f32[6,2048]{1,0:T(8,128)S(1)}) fusion(bf16[6,2,4096,128]{2,3,1,0:T(8,128)(2,1)S(1)} %convolution_bitcast_fusion), kind=kLoop, calls=%fused_computation.9 | loop fusion | flops 18825216 | bytes 12779520 | tf_op jit(solution)/shard_map/qpt,qpt->qp/dot_general | solution.py:68
  38.9 0.6 fusion.39
  39.5 1.0 %fusion.8 = f32[3,2,4096]{2,1,0:T(2,128)S(1)} fusion(s32[4096]{0:T(1024)S(1)} %pad_add_fusion, bf16[3,2,256]{2,0,1:T(4,128)(2,1)S(1)} %pad_maximum_fusion.1), kind=kOutput, calls=%fused_computation.15 | convolution fusion | flops 13631488 | bytes 117760 | tf_op jit(solution)/shard_map/pc,kqc->kqp/dot_general | solution.py:78
  40.6 1.7 %convolution_bitcast_fusion.1 = bf16[2,2,4096,128]{2,3,1,0:T(8,128)(2,1)S(1)} fusion(s32[4096]{0:T(1024)S(1)} %pad_add_fusion, bf16[2,2,128,256]{3,2,1,0:T(8,128)(2,1)S(1)} %get-tuple-element.47), kind=kOutput, calls=%fused_computation.11 | convolution fusion | flops 1074790400 | bytes 4472832 | tf_op jit(solution)/shard_map/pc,qrct->qrpt/dot_general | solution.py:60
  42.3 1.0 %fusion.14 = (f32[2,2048]{1,0:T(2,128)S(1)}, f32[2,2048]{1,0:T(2,128)S(1)}, f32[2,2048]{1,0:T(2,128)S(1)}, f32[2,2048]{1,0:T(2,128)S(1)}) fusion(bf16[2,2,4096,128]{2,3,1,0:T(8,128)(2,1)S(1)} %convolution_bitcast_fusion.1), kind=kLoop, calls=%fused_computation.27 | loop fusion | flops 6275072 | bytes 4259840 | tf_op jit(solution)/shard_map/qpt,qpt->qp/dot_general | solution.py:68
  43.7 0.8 %copy.48 = f32[256,2,128]{2,1,0:T(2,128)} copy(f32[256,2,128]{0,2,1:T(8,128)S(1)} %bitcast.170) | data formatting | bytes 524288 | tf_op jit(solution)/shard_map/reshape | solution.py:126
  44.5 10.6 %all-to-all-start = ((f32[256,2,128]{2,1,0:T(2,128)}), f32[256,2,128]{2,1,0:T(2,128)S(1)}, u32[]{:S(2)}, u32[]{:S(2)}) async-start(f32[256,2,128]{2,1,0:T(2,128)} %copy.48), calls=%async_computation | async-start | bytes 524288 | tf_op jit(solution)/shard_map/all_to_all | solution.py:127
  55.2 0.6 dynamic_slice.3
  55.8 0.7 add_compare_fusion
  56.5 14.0 %all-to-all-done = f32[256,2,128]{2,1,0:T(2,128)S(1)} async-done(((f32[256,2,128]{2,1,0:T(2,128)}), f32[256,2,128]{2,1,0:T(2,128)S(1)}, u32[]{:S(2)}, u32[]{:S(2)}) %all-to-all-start) | async-done | bytes 262176 | tf_op jit(solution)/shard_map/all_to_all | solution.py:127
  71.2 0.7 select_bitcast_fusion
  72.0 0.6 copy.52
  (73 shorter events, 3.9 us)
Async XLA Ops:
  0.6 18.0 %copy-start = (s32[32]{0:T(128)S(1)}, s32[32]{0:T(128)}, u32[]{:S(2)}) copy-start(s32[32]{0:T(128)} %param.6) | copy-start | bytes 388
  0.6 19.9 %copy-start.1 = (s32[4,512]{1,0:T(4,128)S(1)}, s32[4,512]{1,0:T(4,128)}, u32[]{:S(2)}) copy-start(s32[4,512]{1,0:T(4,128)} %param.7) | copy-start | bytes 24580
  0.7 20.7 %copy-start.2 = (s32[4,512]{1,0:T(4,128)S(1)}, s32[4,512]{1,0:T(4,128)}, u32[]{:S(2)}) copy-start(s32[4,512]{1,0:T(4,128)} %param.8) | copy-start | bytes 24580
  9.7 17.6 %collective-permute-start.1 = (bf16[256,128]{1,0:T(8,128)(2,1)S(1)}, bf16[256,128]{1,0:T(8,128)(2,1)S(1)}, u32[]{:S(2)}, u32[]{:S(2)}) collective-permute-start(bf16[256,128]{1,0:T(8,128)(2,1)S(1)} %all_gather.3), channel_id=1, source_target_pairs={{0,252},{4,0},{8,4},{12,8},{16,12},{20,16},{24,20},{28,24},{32,28}... | collective-permute-start | bytes 196616 | tf_op jit(solution)/shard_map/ppermute | solution.py:16
  18.5 8.8 %collective-permute-start = (bf16[256,128]{1,0:T(8,128)(2,1)S(1)}, bf16[256,128]{1,0:T(8,128)(2,1)S(1)}, u32[]{:S(2)}, u32[]{:S(2)}) collective-permute-start(bf16[256,128]{1,0:T(8,128)(2,1)S(1)} %all_gather.3), channel_id=1, source_target_pairs={{0,4},{4,8},{8,12},{12,16},{16,20},{20,24},{24,28},{28,32},{32,36}... | collective-permute-start | bytes 196616 | tf_op jit(solution)/shard_map/ppermute | solution.py:16
  27.4 11.4 %collective-permute-start.3 = (bf16[256,384]{1,0:T(8,128)(2,1)S(1)}, bf16[256,384]{1,0:T(8,128)(2,1)S(1)}, u32[]{:S(2)}, u32[]{:S(2)}) collective-permute-start(bf16[256,384]{1,0:T(8,128)(2,1)S(1)} %constant_dynamic-update-slice_fusion), channel_id=1, source_target_pairs={{0,244},{4,248},{8,252},{12,0},{16,4},{20,8},{24,12},{28,16},{32,2... | collective-permute-start | bytes 589832 | tf_op jit(solution)/shard_map/ppermute | solution.py:16
  27.5 11.2 %collective-permute-start.2 = (bf16[256,384]{1,0:T(8,128)(2,1)S(1)}, bf16[256,384]{1,0:T(8,128)(2,1)S(1)}, u32[]{:S(2)}, u32[]{:S(2)}) collective-permute-start(bf16[256,384]{1,0:T(8,128)(2,1)S(1)} %constant_dynamic-update-slice_fusion), channel_id=1, source_target_pairs={{0,12},{4,16},{8,20},{12,24},{16,28},{20,32},{24,36},{28,40},{32,4... | collective-permute-start | bytes 589832 | tf_op jit(solution)/shard_map/ppermute | solution.py:16
  43.4 11.8 %copy-start.3 = (s32[4]{0:T(128)S(1)}, s32[4]{0:T(128)}, u32[]{:S(2)}) copy-start(s32[4]{0:T(128)} %param.9) | copy-start | bytes 52
  44.5 25.9 %all-to-all-start = ((f32[256,2,128]{2,1,0:T(2,128)}), f32[256,2,128]{2,1,0:T(2,128)S(1)}, u32[]{:S(2)}, u32[]{:S(2)}) async-start(f32[256,2,128]{2,1,0:T(2,128)} %copy.48), calls=%async_computation | async-start | bytes 524288 | tf_op jit(solution)/shard_map/all_to_all | solution.py:127
where the time goes:
time: 72.8 us; the launch traced here: 72.6 us
  starting transfers between devices  22.2 us (30%)
  waiting for transfers between devices  17.3 us (24%)
  other arithmetic  9.15 us (13%)
  matrix products  8.63 us (12%)
  blocking collectives  8.3 us (11%)
  local copies, waits for them, and re-layouts  5.9 us (8%)
  between operations  1.14 us (2%)
    all_to_all x1, waiting for transfers between devices, shards(): exchanged = lax.all_to_all(partial_value, ('tm', 'chan'), 0, 0, tiled=True)  14 us
    ppermute x4, starting transfers between devices, from_behind(): lax.ppermute(array, axis, [(i, (i + by) % peers) for i in range(peers)])  11.5 us
    all_to_all x1, starting transfers between devices, shards(): exchanged = lax.all_to_all(partial_value, ('tm', 'chan'), 0, 0, tiled=True)  10.6 us
    all_gather x1, blocking collectives, shards(): gathered = lax.all_gather(rounded, 'chan', axis=0, tiled=True)  8.3 us
    dot_general x2, matrix products, pair_sums(): jnp.einsum('pc,qrct->qrpt', pick, parts, preferred_element_type=jnp.bfloa...  5.6 us
    dot_general x2, other arithmetic, time_sum(): jnp.einsum('qpt,qpt->qp', left, right, preferred_element_type=jnp.float32)  4.04 us
    ppermute x4, waiting for transfers between devices, from_behind(): lax.ppermute(array, axis, [(i, (i + by) % peers) for i in range(peers)])  3.3 us
    dot_general x2, matrix products, pair_sums(): jnp.einsum('pc,kqc->kqp', pick, pieces, preferred_element_type=jnp.float32)  1.86 us
  transfers between devices with their start and end apart: 5, of which 2 were waited for; matrix products, arithmetic and copies ran while one was open for 21% of the time, Pallas kernels for 0%

commit v1 on v0

--- a/solution.py
+++ b/solution.py
@@ -90,7 +90,9 @@
     time_span = signal.shape[1]
     ntime = time_span * time_devices
     rounded = signal.astype(jnp.bfloat16)
-    gathered = lax.all_gather(rounded, "chan", axis=0, tiled=True)
+    gathered = jnp.concatenate(
+        lax.all_to_all(jnp.stack([rounded] * lax.axis_size("chan")), "chan", 0, 0), axis=0
+    )
     near = jnp.concatenate(
         [from_behind(gathered, "tm", 1), gathered, from_behind(gathered, "tm", -1)], axis=1
     )

time: 72.8 us -> 77.1 us (1.059)
  blocking collectives: 8.3 us -> 0 us
  starting transfers between devices: 22.2 us -> 28.5 us
  waiting for transfers between devices: 17.3 us -> 23 us
    all_gather x1 -> x0, blocking collectives: 8.3 us -> none  [shards(): gathered = lax.all_gather(rounded, 'chan', axis=0, tiled=True)]
    all_to_all x0 -> x1, starting transfers between devices: none -> 6.49 us  [shards(): lax.all_to_all(jnp.stack([rounded] * lax.axis_size('chan')), 'chan', 0, 0)]
    ppermute x4, waiting for transfers between devices: 3.3 us -> 8.84 us  [from_behind(): lax.ppermute(array, axis, [(i, (i + by) % peers) for i in range(peers)])]
    all_to_all x1, starting transfers between devices: 10.6 us -> 7.09 us  [shards(): exchanged = lax.all_to_all(partial_value, ('tm', 'chan'), 0, 0, tiled=True)]
    ppermute x4, starting transfers between devices: 11.5 us -> 14.9 us  [from_behind(): lax.ppermute(array, axis, [(i, (i + by) % peers) for i in range(peers)])]
  transfers between devices with their start and end apart: 5 -> 6, of which waited for: 2 -> 3; matrix products, arithmetic and copies ran while one was open for 21% -> 20% of each run, Pallas kernels for 0% -> 0%
where the time goes in v1:
time: 77.1 us; the launch traced here: 76.8 us
  starting transfers between devices  28.5 us (37%)
  waiting for transfers between devices  23 us (30%)
  other arithmetic  9.16 us (12%)
  matrix products  8.62 us (11%)
  local copies, waits for them, and re-layouts  6.49 us (8%)
  between operations  1.13 us (1%)
    ppermute x4, starting transfers between devices, from_behind(): lax.ppermute(array, axis, [(i, (i + by) % peers) for i in range(peers)])  14.9 us
    all_to_all x1, waiting for transfers between devices, shards(): exchanged = lax.all_to_all(partial_value, ('tm', 'chan'), 0, 0, tiled=True)  14.1 us
    ppermute x4, waiting for transfers between devices, from_behind(): lax.ppermute(array, axis, [(i, (i + by) % peers) for i in range(peers)])  8.84 us
    all_to_all x1, starting transfers between devices, shards(): exchanged = lax.all_to_all(partial_value, ('tm', 'chan'), 0, 0, tiled=True)  7.09 us
    all_to_all x1, starting transfers between devices, shards(): lax.all_to_all(jnp.stack([rounded] * lax.axis_size('chan')), 'chan', 0, 0)  6.49 us
    dot_general x2, matrix products, pair_sums(): jnp.einsum('pc,qrct->qrpt', pick, parts, preferred_element_type=jnp.bfloa...  5.59 us
    dot_general x2, other arithmetic, time_sum(): jnp.einsum('qpt,qpt->qp', left, right, preferred_element_type=jnp.float32)  4.04 us
    dot_general x2, matrix products, pair_sums(): jnp.einsum('pc,kqc->kqp', pick, pieces, preferred_element_type=jnp.float32)  1.86 us
  transfers between devices with their start and end apart: 6, of which 3 were waited for; matrix products, arithmetic and copies ran while one was open for 20% of the time, Pallas kernels for 0%

profile of v1, /device:TPU:1, one launch (start us, length us, event | category | flops | bytes accessed | tf_op | source)
XLA Modules:
  0.0 76.8 jit_solution(15301509758227744940)
XLA Ops:
  0.6 0.8 convert_element_type.133
  1.4 0.6 stack.89
  2.0 6.5 %all-to-all-start = ((bf16[4,64,128]{2,1,0:T(8,128)(2,1)}), bf16[4,64,128]{2,1,0:T(8,128)(2,1)S(1)}, u32[]{:S(2)}, u32[]{:S(2)}) async-start(bf16[4,64,128]{2,1,0:T(8,128)(2,1)} %stack.89), calls=%async_computation | async-start | bytes 131072 | tf_op jit(solution)/shard_map/all_to_all | solution.py:94
  8.7 0.6 gather_fusion.1
  9.3 0.6 gather_fusion
  10.7 1.0 %fusion.27 = (bf16[2,1,1152,128]{2,3,1,0:T(8,128)(2,1)S(1)}, bf16[2,1,1152,128]{2,3,1,0:T(8,128)(2,1)S(1)}) fusion(f32[2,128]{1,0:T(2,128)S(1)} %get-tuple-element.45, f32[2,1152]{1,0:T(2,128)S(1)} %get-tuple-element.29, f32[2,128]{1,0:T(2,128)S(1)} %get-tuple-element.44, f32[2,1152]{1,0:T(2,128)S(1)} %get-tuple-element.28, f32[2]{0:T(128)S(1)} %get-tuple-element.51, ...), kind=kLoop, calls=%fused_computation.49 | loop fusion | flops 5013504 | bytes 2379800 | tf_op jit(solution)/shard_map/convert_element_type | solution.py:39
  11.7 0.8 %fusion.25 = (bf16[6,1,384,128]{2,3,1,0:T(8,128)(2,1)S(1)}, bf16[6,1,384,128]{2,3,1,0:T(8,128)(2,1)S(1)}) fusion(f32[6,128]{1,0:T(8,128)S(1)} %get-tuple-element.43, f32[6,384]{1,0:T(8,128)S(1)} %get-tuple-element.36, f32[6,128]{1,0:T(8,128)S(1)} %get-tuple-element.42, f32[6,384]{1,0:T(8,128)S(1)} %get-tuple-element.35, f32[6]{0:T(128)S(1)} %get-tuple-element.55, ...), kind=kLoop, calls=%fused_computation.47 | loop fusion | flops 5013504 | bytes 1597512 | tf_op jit(solution)/shard_map/convert_element_type | solution.py:39
  14.1 8.8 %collective-permute-start.1 = (bf16[256,128]{1,0:T(8,128)(2,1)S(1)}, bf16[256,128]{1,0:T(8,128)(2,1)S(1)}, u32[]{:S(2)}, u32[]{:S(2)}) collective-permute-start(bf16[256,128]{1,0:T(8,128)(2,1)S(1)} %bitcast.172), channel_id=1, source_target_pairs={{0,252},{4,0},{8,4},{12,8},{16,12},{20,16},{24,20},{28,24},{32,28}... | collective-permute-start | bytes 196616 | tf_op jit(solution)/shard_map/ppermute | solution.py:16
  22.9 1.3 %collective-permute-done.1 = bf16[256,128]{1,0:T(8,128)(2,1)S(1)} collective-permute-done((bf16[256,128]{1,0:T(8,128)(2,1)S(1)}, bf16[256,128]{1,0:T(8,128)(2,1)S(1)}, u32[]{:S(2)}, u32[]{:S(2)}) %collective-permute-start.1) | collective-permute-done | bytes 65568 | tf_op jit(solution)/shard_map/ppermute | solution.py:16
  24.3 7.5 %collective-permute-done = bf16[256,128]{1,0:T(8,128)(2,1)S(1)} collective-permute-done((bf16[256,128]{1,0:T(8,128)(2,1)S(1)}, bf16[256,128]{1,0:T(8,128)(2,1)S(1)}, u32[]{:S(2)}, u32[]{:S(2)}) %collective-permute-start) | collective-permute-done | bytes 65568 | tf_op jit(solution)/shard_map/ppermute | solution.py:16
  31.9 6.0 %collective-permute-start.3 = (bf16[256,384]{1,0:T(8,128)(2,1)S(1)}, bf16[256,384]{1,0:T(8,128)(2,1)S(1)}, u32[]{:S(2)}, u32[]{:S(2)}) collective-permute-start(bf16[256,384]{1,0:T(8,128)(2,1)S(1)} %pad_maximum_fusion), channel_id=1, source_target_pairs={{0,244},{4,248},{8,252},{12,0},{16,4},{20,8},{24,12},{28,16},{32,2... | collective-permute-start | bytes 589832 | tf_op jit(solution)/shard_map/ppermute | solution.py:16
  37.9 0.6 fusion.20
  38.5 0.8 %fusion.10 = f32[3,6,4096]{2,1,0:T(8,128)S(1)} fusion(s32[4096]{0:T(1024)S(1)} %pad_add_fusion, bf16[1,6,256]{2,1,0:T(8,128)(2,1)S(1)} %get-tuple-element.31, bf16[1,6,256]{2,1,0:T(8,128)(2,1)S(1)} %get-tuple-element.32, bf16[1,6,256]{2,1,0:T(8,128)(2,1)S(1)} %get-tuple-element.30), kind=kOutput, calls=%fused_computation.16 | convolution fusion | flops 38806528 | bytes 320512 | tf_op jit(solution)/shard_map/pc,kqc->kqp/dot_general | solution.py:78
  39.4 3.9 %convolution_bitcast_fusion = bf16[6,2,4096,128]{2,3,1,0:T(8,128)(2,1)S(1)} fusion(s32[4096]{0:T(1024)S(1)} %pad_add_fusion, bf16[6,2,128,256]{3,2,1,0:T(8,128)(2,1)S(1)} %get-tuple-element.49), kind=kOutput, calls=%fused_computation.6 | convolution fusion | flops 3222274048 | bytes 13385728 | tf_op jit(solution)/shard_map/pc,qrct->qrpt/dot_general | solution.py:60
  43.3 3.1 %fusion.2 = (f32[6,2048]{1,0:T(8,128)S(1)}, f32[6,2048]{1,0:T(8,128)S(1)}, f32[6,2048]{1,0:T(8,128)S(1)}, f32[6,2048]{1,0:T(8,128)S(1)}) fusion(bf16[6,2,4096,128]{2,3,1,0:T(8,128)(2,1)S(1)} %convolution_bitcast_fusion), kind=kLoop, calls=%fused_computation.9 | loop fusion | flops 18825216 | bytes 12779520 | tf_op jit(solution)/shard_map/qpt,qpt->qp/dot_general | solution.py:68
  47.2 1.0 %fusion.8 = f32[3,2,4096]{2,1,0:T(2,128)S(1)} fusion(s32[4096]{0:T(1024)S(1)} %pad_add_fusion, bf16[3,2,256]{2,0,1:T(4,128)(2,1)S(1)} %pad_maximum_fusion.2), kind=kOutput, calls=%fused_computation.15 | convolution fusion | flops 13631488 | bytes 117760 | tf_op jit(solution)/shard_map/pc,kqc->kqp/dot_general | solution.py:78
  48.3 1.7 %convolution_bitcast_fusion.1 = bf16[2,2,4096,128]{2,3,1,0:T(8,128)(2,1)S(1)} fusion(s32[4096]{0:T(1024)S(1)} %pad_add_fusion, bf16[2,2,128,256]{3,2,1,0:T(8,128)(2,1)S(1)} %get-tuple-element.47), kind=kOutput, calls=%fused_computation.11 | convolution fusion | flops 1074790400 | bytes 4472832 | tf_op jit(solution)/shard_map/pc,qrct->qrpt/dot_general | solution.py:60
  50.0 1.0 %fusion.14 = (f32[2,2048]{1,0:T(2,128)S(1)}, f32[2,2048]{1,0:T(2,128)S(1)}, f32[2,2048]{1,0:T(2,128)S(1)}, f32[2,2048]{1,0:T(2,128)S(1)}) fusion(bf16[2,2,4096,128]{2,3,1,0:T(8,128)(2,1)S(1)} %convolution_bitcast_fusion.1), kind=kLoop, calls=%fused_computation.27 | loop fusion | flops 6275072 | bytes 4259840 | tf_op jit(solution)/shard_map/qpt,qpt->qp/dot_general | solution.py:68
  51.4 0.8 %copy.48 = f32[256,2,128]{2,1,0:T(2,128)} copy(f32[256,2,128]{0,2,1:T(8,128)S(1)} %bitcast.171) | data formatting | bytes 524288 | tf_op jit(solution)/shard_map/reshape | solution.py:128
  52.2 7.1 %all-to-all-start.1 = ((f32[256,2,128]{2,1,0:T(2,128)}), f32[256,2,128]{2,1,0:T(2,128)S(1)}, u32[]{:S(2)}, u32[]{:S(2)}) async-start(f32[256,2,128]{2,1,0:T(2,128)} %copy.48), calls=%async_computation.1 | async-start | bytes 524288 | tf_op jit(solution)/shard_map/all_to_all | solution.py:129
  59.9 0.7 add_compare_fusion
  60.6 14.1 %all-to-all-done.1 = f32[256,2,128]{2,1,0:T(2,128)S(1)} async-done(((f32[256,2,128]{2,1,0:T(2,128)}), f32[256,2,128]{2,1,0:T(2,128)S(1)}, u32[]{:S(2)}, u32[]{:S(2)}) %all-to-all-start.1) | async-done | bytes 262176 | tf_op jit(solution)/shard_map/all_to_all | solution.py:129
  75.5 0.7 select_bitcast_fusion
  76.2 0.6 copy.52
  (73 shorter events, 5.1 us)
Async XLA Ops:
  0.6 8.0 %copy-start = (s32[32]{0:T(128)S(1)}, s32[32]{0:T(128)}, u32[]{:S(2)}) copy-start(s32[32]{0:T(128)} %param.6) | copy-start | bytes 388
  2.0 12.0 %all-to-all-start = ((bf16[4,64,128]{2,1,0:T(8,128)(2,1)}), bf16[4,64,128]{2,1,0:T(8,128)(2,1)S(1)}, u32[]{:S(2)}, u32[]{:S(2)}) async-start(bf16[4,64,128]{2,1,0:T(8,128)(2,1)} %stack.89), calls=%async_computation | async-start | bytes 131072 | tf_op jit(solution)/shard_map/all_to_all | solution.py:94
  11.7 0.8 %copy-start.1 = (s32[4,512]{1,0:T(4,128)S(1)}, s32[4,512]{1,0:T(4,128)}, u32[]{:S(2)}) copy-start(s32[4,512]{1,0:T(4,128)} %param.7) | copy-start | bytes 24580
  11.7 1.6 %copy-start.2 = (s32[4,512]{1,0:T(4,128)S(1)}, s32[4,512]{1,0:T(4,128)}, u32[]{:S(2)}) copy-start(s32[4,512]{1,0:T(4,128)} %param.8) | copy-start | bytes 24580
  14.1 10.2 %collective-permute-start.1 = (bf16[256,128]{1,0:T(8,128)(2,1)S(1)}, bf16[256,128]{1,0:T(8,128)(2,1)S(1)}, u32[]{:S(2)}, u32[]{:S(2)}) collective-permute-start(bf16[256,128]{1,0:T(8,128)(2,1)S(1)} %bitcast.172), channel_id=1, source_target_pairs={{0,252},{4,0},{8,4},{12,8},{16,12},{20,16},{24,20},{28,24},{32,28}... | collective-permute-start | bytes 196616 | tf_op jit(solution)/shard_map/ppermute | solution.py:16
  22.9 8.8 %collective-permute-start = (bf16[256,128]{1,0:T(8,128)(2,1)S(1)}, bf16[256,128]{1,0:T(8,128)(2,1)S(1)}, u32[]{:S(2)}, u32[]{:S(2)}) collective-permute-start(bf16[256,128]{1,0:T(8,128)(2,1)S(1)} %bitcast.173), channel_id=1, source_target_pairs={{0,4},{4,8},{8,12},{12,16},{16,20},{20,24},{24,28},{28,32},{32,36}... | collective-permute-start | bytes 196616 | tf_op jit(solution)/shard_map/ppermute | solution.py:16
  31.8 14.6 %collective-permute-start.2 = (bf16[256,384]{1,0:T(8,128)(2,1)S(1)}, bf16[256,384]{1,0:T(8,128)(2,1)S(1)}, u32[]{:S(2)}, u32[]{:S(2)}) collective-permute-start(bf16[256,384]{1,0:T(8,128)(2,1)S(1)} %pad_maximum_fusion), channel_id=1, source_target_pairs={{0,12},{4,16},{8,20},{12,24},{16,28},{20,32},{24,36},{28,40},{32,4... | collective-permute-start | bytes 589832 | tf_op jit(solution)/shard_map/ppermute | solution.py:16
  31.9 14.6 %collective-permute-start.3 = (bf16[256,384]{1,0:T(8,128)(2,1)S(1)}, bf16[256,384]{1,0:T(8,128)(2,1)S(1)}, u32[]{:S(2)}, u32[]{:S(2)}) collective-permute-start(bf16[256,384]{1,0:T(8,128)(2,1)S(1)} %pad_maximum_fusion), channel_id=1, source_target_pairs={{0,244},{4,248},{8,252},{12,0},{16,4},{20,8},{24,12},{28,16},{32,2... | collective-permute-start | bytes 589832 | tf_op jit(solution)/shard_map/ppermute | solution.py:16
  51.1 8.3 %copy-start.3 = (s32[4]{0:T(128)S(1)}, s32[4]{0:T(128)}, u32[]{:S(2)}) copy-start(s32[4]{0:T(128)} %param.9) | copy-start | bytes 52
  52.2 22.5 %all-to-all-start.1 = ((f32[256,2,128]{2,1,0:T(2,128)}), f32[256,2,128]{2,1,0:T(2,128)S(1)}, u32[]{:S(2)}, u32[]{:S(2)}) async-start(f32[256,2,128]{2,1,0:T(2,128)} %copy.48), calls=%async_computation.1 | async-start | bytes 524288 | tf_op jit(solution)/shard_map/all_to_all | solution.py:129
